TPU v7x, 32 devices: a whole 2x2x4 slice. The times are simulated.
32 devices in a mesh: row: 2 (over core), col: 2 (over x), seq: 8 (over z, y).
Axes of the slice: x: 2, y: 2, z: 4, core: 2. Of those that a mesh axis runs over, the one named last changes fastest.
Arguments:
- states: bfloat16 [128, 4, 5120], P('col', None, 'row'), may hold values from -64 to 64
- norm_gain: float32 [5120], P('row'), may hold values from 0.1 to 1.9
- wq: bfloat16 [5120, 4096], P('row', 'col'), may hold values from -0.078125 to 0.078125
- wk: bfloat16 [5120, 1024], P('row', 'col'), may hold values from -0.21875 to 0.21875
- wv: bfloat16 [5120, 1024], P('row', 'col'), may hold values from -0.078125 to 0.078125
- wo: bfloat16 [4096, 5120], P('col', 'row'), may hold values from -0.09375 to 0.09375
- lengths: int32 [128], P('row'), may hold values from 1 to 8192, as said below
- slot_request: int32 [800], P(('row', 'seq')), may hold values from 0 to 64, as said below
- slot_block_number: int32 [800], P(('row', 'seq')), may hold values from 0 to 63, as said below
- paged_key_cache: bfloat16 [800, 128, 1024], P(('row', 'seq'), None, 'col'), may hold values from -120 to 120
- paged_value_cache: bfloat16 [800, 128, 1024], P(('row', 'seq'), None, 'col'), may hold values from -6 to 6
Outputs:
- attended: bfloat16 [128, 4, 5120], P('col', None, 'row')
- new_keys: bfloat16 [128, 4, 1024], P('row', None, 'col')
- new_values: bfloat16 [128, 4, 1024], P('row', None, 'col')
Inputs may be any that keep to these rules, and one draw needn't show every extreme that they name: `lengths`: within every 64 consecutive requests, 8 have exactly 8192 cached tokens and the others fewer than 128. `slot_request`: each request's block 0 and every block that holds a position visible to one of its steps stand in exactly one slot of its index of row; a long request has exactly 33 slots. 64 marks an empty slot; every index of row has empty slots. `slot_block_number`: 0 in empty slots.
All inputs are finite; a program needn't handle non-finite values.
Results may differ from a plain program's by a relative error of at most 0.034.
Values may be sent and summed in bfloat16 or wider, within the bound.
No kernel may reach another device: no remote copies, remote signals or barrier semaphores. Data moves between devices by JAX's collectives and lax.ppermute only.
A program may use at most 192 MiB of HBM per device.

v0:
```python
import math
import jax
import jax.numpy as jnp
from jax import lax
from jax.sharding import PartitionSpec as P

D = 5120
HEAD_SIZE = 128
WINDOW = 4096
SINK = 4
QUERY_PER_KEY = 4
EPSILON = 1e-05
NEGATIVE_FILL = -1e30
ROPE_BASE = 100000000.0


def rotary_apply(values, token_positions):
    half_dim = values.shape[-1] // 2
    frequency = ROPE_BASE ** (-(jnp.arange(half_dim, dtype=jnp.float32) * 2.0 / values.shape[-1]))
    angles = (token_positions.astype(jnp.float32)[..., None] * frequency)[..., None, :]
    cosine = jnp.cos(angles)
    sine_part = jnp.sin(angles)
    lower = values[..., :half_dim]
    upper = values[..., half_dim:]
    return jnp.concatenate(
        [lower * cosine - upper * sine_part, upper * cosine + lower * sine_part], -1
    )


def slot_parts(query_rows, lengths, slot_request, slot_block_number, key_rows, value_rows):
    req_count = query_rows.shape[0]
    step_count = query_rows.shape[1]
    block_len = key_rows.shape[1]
    picked = jnp.minimum(slot_request, req_count - 1)
    in_use = slot_request < req_count
    slot_queries = query_rows[picked]
    scores = jnp.einsum(
        "nsagh,nbah->nasgb", slot_queries, key_rows, preferred_element_type=jnp.float32
    ) * (1.0 / math.sqrt(HEAD_SIZE))
    key_pos = (
        slot_block_number[:, None] * block_len + jnp.arange(block_len, dtype=jnp.int32)[None, :]
    )
    own_len = lengths[picked]
    query_pos = own_len[:, None] + jnp.arange(step_count, dtype=jnp.int32)[None, :]
    visible = (
        in_use[:, None, None]
        & (key_pos[:, None, :] < own_len[:, None, None])
        & ((key_pos[:, None, :] < SINK) | (key_pos[:, None, :] > query_pos[:, :, None] - WINDOW))
    )
    visible = visible[:, None, :, None, :]
    slot_peak = jnp.max(jnp.where(visible, scores, NEGATIVE_FILL), -1)
    weights = jnp.where(visible, jnp.exp(scores - slot_peak[..., None]), 0.0)
    slot_total = jnp.sum(weights, -1)
    slot_acc = jnp.einsum(
        "nasgb,nbah->nasgh",
        weights.astype(jnp.bfloat16),
        value_rows,
        preferred_element_type=jnp.float32,
    )
    member = slot_request[None, :] == jnp.arange(req_count, dtype=jnp.int32)[:, None]
    local_peak = jnp.max(
        jnp.where(member[:, :, None, None, None], slot_peak[None], NEGATIVE_FILL), 1
    )
    return (local_peak, (slot_peak, slot_total, slot_acc, member, picked))


def pool_sums(held, running_peak):
    slot_peak, slot_total, slot_acc, member, picked = held
    factor = jnp.exp(slot_peak - running_peak[picked])
    as_member = member.astype(jnp.float32)
    running_totals = jnp.einsum(
        "rn,nasg->rasg", as_member, slot_total * factor, precision=lax.Precision.HIGHEST
    )
    weighted_values = jnp.einsum(
        "rn,nasgh->rasgh", as_member, slot_acc * factor[..., None], precision=lax.Precision.HIGHEST
    )
    return (running_totals, weighted_values)


def fresh_part(query_rows, key_all, value_all):
    step_count = query_rows.shape[1]
    used = key_all.shape[1]
    scores = jnp.einsum(
        "rsagh,ruah->rasgu", query_rows, key_all, preferred_element_type=jnp.float32
    ) * (1.0 / math.sqrt(HEAD_SIZE))
    causal = (
        jnp.arange(used, dtype=jnp.int32)[None, :]
        <= jnp.arange(step_count, dtype=jnp.int32)[:, None]
    )
    causal = causal[None, None, :, None, :]
    running_peak = jnp.max(jnp.where(causal, scores, NEGATIVE_FILL), -1)
    weights = jnp.where(causal, jnp.exp(scores - running_peak[..., None]), 0.0)
    running_totals = jnp.sum(weights, -1)
    weighted_values = jnp.einsum(
        "rasgu,ruah->rasgh",
        weights.astype(jnp.bfloat16),
        value_all,
        preferred_element_type=jnp.float32,
    )
    return (running_peak, running_totals, weighted_values)


def merge_parts(earlier, later):
    running_peak = jnp.maximum(earlier[0], later[0])
    first_factor = jnp.exp(earlier[0] - running_peak)
    second_factor = jnp.exp(later[0] - running_peak)
    running_totals = earlier[1] * first_factor + later[1] * second_factor
    weighted_values = earlier[2] * first_factor[..., None] + later[2] * second_factor[..., None]
    return (running_peak, running_totals, weighted_values)


def seq_merge(peak, total, acc, n_seq, seq_index):
    stages = n_seq.bit_length() - 1
    assert 1 << stages == n_seq
    req_count = peak.shape[0]
    per = req_count // n_seq
    rest = peak.shape[1:]
    split = [2] * stages + [per]
    stats = jnp.stack([peak, total], 0).reshape([2] + split + list(rest))
    values = acc.reshape(split + list(acc.shape[1:]))
    for bit in range(stages):
        axis = stages - 1 - bit
        mine = seq_index >> bit & 1
        pairs = [(s, s ^ 1 << bit) for s in range(n_seq)]
        keep_stats = lax.dynamic_index_in_dim(stats, mine, axis + 1, keepdims=True)
        send_stats = lax.dynamic_index_in_dim(stats, 1 - mine, axis + 1, keepdims=True)
        keep_values = lax.dynamic_index_in_dim(values, mine, axis, keepdims=True)
        send_values = lax.dynamic_index_in_dim(values, 1 - mine, axis, keepdims=True)
        got_stats = lax.ppermute(send_stats, "seq", pairs)
        got_values = lax.ppermute(send_values.astype(jnp.bfloat16), "seq", pairs).astype(
            jnp.float32
        )
        top = jnp.maximum(keep_stats[0], got_stats[0])
        keep_factor = jnp.exp(keep_stats[0] - top)
        got_factor = jnp.exp(got_stats[0] - top)
        stats = jnp.stack([top, keep_stats[1] * keep_factor + got_stats[1] * got_factor], 0)
        values = keep_values * keep_factor[..., None] + got_values * got_factor[..., None]
    stats = stats.reshape((2, per) + tuple(rest))
    values = values.reshape((per,) + tuple(acc.shape[1:]))
    return (stats[0], stats[1], values)


def on_device(
    states,
    norm_gain,
    wq,
    wk,
    wv,
    wo,
    lengths,
    slot_request,
    slot_block_number,
    paged_key_cache,
    paged_value_cache,
):
    q_width = wq.shape[1]
    k_width = wk.shape[1]
    heads_kv = k_width // HEAD_SIZE
    req_count = lengths.shape[0]
    block_len = paged_key_cache.shape[1]
    key_rows = paged_key_cache.reshape(paged_key_cache.shape[0], block_len, heads_kv, HEAD_SIZE)
    value_rows = paged_value_cache.reshape(
        paged_value_cache.shape[0], block_len, heads_kv, HEAD_SIZE
    )
    step_count = states.shape[1]
    as_float = states.astype(jnp.float32)
    squares = lax.psum(jnp.sum(as_float * as_float, -1), "row")
    normed = (as_float * lax.rsqrt(squares / D + EPSILON)[..., None] * norm_gain).astype(
        jnp.bfloat16
    )
    gathered = lax.all_gather(normed, "col", axis=0, tiled=True)
    piece_rows = gathered.reshape(req_count * lax.axis_size("row") * step_count, -1)
    parts_out = [
        jnp.dot(piece_rows, matrix, preferred_element_type=jnp.float32) for matrix in (wq, wk, wv)
    ]
    output_projected = lax.psum_scatter(
        jnp.concatenate(parts_out, axis=-1)
        .reshape(req_count * lax.axis_size("row"), step_count, -1)
        .astype(jnp.bfloat16),
        "row",
        scatter_dimension=0,
        tiled=True,
    ).astype(jnp.float32)
    token_positions = lengths[:, None] + jnp.arange(step_count, dtype=jnp.int32)[None, :]
    query_rows = rotary_apply(
        output_projected[..., :q_width].reshape(req_count, step_count, -1, HEAD_SIZE),
        token_positions,
    ).astype(jnp.bfloat16)
    query_rows = query_rows.reshape(req_count, step_count, heads_kv, QUERY_PER_KEY, HEAD_SIZE)
    current_key = rotary_apply(
        output_projected[..., q_width : q_width + k_width].reshape(
            req_count, step_count, heads_kv, HEAD_SIZE
        ),
        token_positions,
    ).astype(jnp.bfloat16)
    current_value = (
        output_projected[..., q_width + k_width :]
        .reshape(req_count, step_count, heads_kv, HEAD_SIZE)
        .astype(jnp.bfloat16)
    )
    local_peak, held = slot_parts(
        query_rows, lengths, slot_request, slot_block_number, key_rows, value_rows
    )
    local_totals, local_values = pool_sums(held, local_peak)
    n_seq = lax.axis_size("seq")
    per = req_count // n_seq
    seq_index = lax.axis_index("seq")
    mine = seq_index * per
    running_peak, running_totals, weighted_values = seq_merge(
        local_peak, local_totals, local_values, n_seq, seq_index
    )
    own_queries = lax.dynamic_slice_in_dim(query_rows, mine, per, 0)
    fresh = fresh_part(
        own_queries,
        lax.dynamic_slice_in_dim(current_key, mine, per, 0),
        lax.dynamic_slice_in_dim(current_value, mine, per, 0),
    )
    running_peak, running_totals, weighted_values = merge_parts(
        (running_peak, running_totals, weighted_values), fresh
    )
    heads_out = (
        (weighted_values / running_totals[..., None])
        .transpose(0, 2, 1, 3, 4)
        .reshape(per, step_count, -1)
        .astype(jnp.bfloat16)
    )
    piece_rows = lax.all_gather(heads_out, "row", axis=0, tiled=False)
    n_row = piece_rows.shape[0]
    product = jnp.dot(
        piece_rows.reshape(n_row * per * step_count, -1), wo, preferred_element_type=jnp.float32
    )
    partials = product.reshape(n_row, per, step_count, -1)
    own_out = lax.psum_scatter(
        partials.astype(jnp.bfloat16), "col", scatter_dimension=0, tiled=True
    ).reshape(per, step_count, -1)
    attended = lax.all_gather(own_out, "seq", axis=0, tiled=True)
    return (
        attended,
        current_key.reshape(req_count, step_count, k_width),
        current_value.reshape(req_count, step_count, k_width),
    )


def solution(mesh):
    in_specs = (
        P("col", None, "row"),
        P("row"),
        P("row", "col"),
        P("row", "col"),
        P("row", "col"),
        P("col", "row"),
        P("row"),
        P(("row", "seq")),
        P(("row", "seq")),
        P(("row", "seq"), None, "col"),
        P(("row", "seq"), None, "col"),
    )
    out_specs = (P("col", None, "row"), P("row", None, "col"), P("row", None, "col"))
    return jax.shard_map(
        on_device, mesh=mesh, in_specs=in_specs, out_specs=out_specs, check_vma=False
    )
```

profile of v0, /device:TPU:0, one launch (start us, length us, event | category | flops | bytes accessed | tf_op | source)
XLA Modules:
  0.0 265.6 jit_solution(17505629479722814669)
XLA Ops:
  7.2 2.2 fusion.9
  9.5 2.6 psum.7
  12.2 3.1 %fusion.11 = bf16[64,4,2560]{2,1,0:T(4,128)(2,1)} fusion(bf16[64,4,2560]{2,1,0:T(4,128)(2,1)} %param.11, f32[2560]{0:T(1024)} %param.12, f32[64,4]{1,0:T(8,128)S(1)} %copy.273), kind=kLoop, calls=%fused_computation.16 | loop fusion | flops 2621440 | bytes 2632704 | tf_op jit(solution)/shard_map/convert_element_type | solution.py:168
  15.4 41.7 %all-gather.4.cloned.1.call-done = bf16[128,4,2560]{2,1,0:T(4,128)(2,1)} async-done(((bf16[64,4,2560]{2,1,0:T(4,128)(2,1)}), bf16[128,4,2560]{2,1,0:T(4,128)(2,1)}) %all-gather.4.cloned.1.call-update) | async-done | bytes 2621456 | tf_op jit(solution)/shard_map/all_gather | solution.py:171
  57.1 5.3 %reshape.465 = bf16[512,2560]{1,0:T(8,128)(2,1)} reshape(bf16[128,4,2560]{2,1,0:T(4,128)(2,1)} %all-gather.4.cloned.1.call-done) | data formatting | bytes 5242880 | tf_op jit(solution)/shard_map/reshape | solution.py:172
  62.5 3.4 %convolution_convert_fusion.1 = bf16[512,512]{1,0:T(8,128)(2,1)S(1)} fusion(bf16[512,2560]{1,0:T(8,128)(2,1)} %reshape.465, bf16[2560,512]{1,0:T(8,128)(2,1)S(1)} %copy-done), kind=kOutput, calls=%fused_computation.26 | convolution fusion | flops 1342439424 | bytes 5767168 | tf_op jit(solution)/shard_map/dot_general | solution.py:174
  65.9 1.5 convolution_convert_fusion.2
  67.4 8.5 %convolution_convert_fusion = bf16[512,2048]{1,0:T(8,128)(2,1)S(1)} fusion(bf16[512,2560]{1,0:T(8,128)(2,1)S(1)} %copy-done.5, bf16[2560,2048]{1,0:T(8,128)(2,1)} %param.13), kind=kOutput, calls=%fused_computation.13 | convolution fusion | flops 5369757696 | bytes 15204352 | tf_op jit(solution)/shard_map/dot_general | solution.py:174
  75.9 1.8 pad_maximum_fusion
  77.7 6.1 %convert_element_type.83 = bf16[128,4,3072]{2,1,0:T(4,128)(2,1)} reshape(bf16[512,3072]{1,0:T(8,128)(2,1)} %pad_maximum_fusion) | data formatting | bytes 6291456 | tf_op jit(solution)/shard_map/convert_element_type | solution.py:179
  84.5 0.8 gather_fusion
  85.4 1.1 multiply_cosine_fusion
  86.5 12.4 %reshape.467 = bf16[50,128,4,128]{3,2,1,0:T(4,128)(2,1)} reshape(bf16[50,128,512]{2,1,0:T(8,128)(2,1)} %param.20) | data formatting | bytes 13107200 | tf_op jit(solution)/shard_map/reshape | solution.py:161
  98.9 12.4 %reshape.468 = bf16[50,128,4,128]{3,2,1,0:T(4,128)(2,1)} reshape(bf16[50,128,512]{2,1,0:T(8,128)(2,1)} %param.21) | data formatting | bytes 13107200 | tf_op jit(solution)/shard_map/reshape | solution.py:162
  111.2 0.6 dynamic-slice
  113.0 1.8 dynamic-slice_convert_fusion
  114.8 0.9 slice_bitcast_fusion.2
  115.8 0.8 copy-done.3
  116.6 1.5 slice.92
  118.1 2.3 reshape.509
  120.4 0.7 fusion.76
  121.2 0.6 subtract_convert_fusion
  121.7 1.4 pad_maximum_fusion.1
  123.2 0.6 copy.329
  123.7 2.2 gather_fusion.1
  125.9 7.9 %select_reduce_fusion.1 = (f32[50,4,4,4]{3,2,1,0:T(4,128)S(1)}, f32[50,4,4,4,128]{4,3,2,1,0:T(4,128)}) fusion(pred[50,4,128]{2,1,0:T(4,128)(4,1)S(1)} %or_and_fusion, bf16[50,4,4,4,128]{4,3,1,2,0:T(4,128)(2,1)} %gather_fusion.1, bf16[50,128,4,128,1]{3,2,1,0,4:T(4,128)(2,1)} %bitcast.123), kind=kOutput, calls=%fused_computation.23 | convolution fusion | flops 106083200 | bytes 9049600 | tf_op jit(solution)/shard_map/nsagh,nbah->nasgb/dot_general | solution.py:37
  133.9 1.3 select_reduce_fusion
  135.1 1.1 stack.10
  136.6 0.5 multiply_subtract_fusion
  137.4 1.2 fusion.36
  138.7 0.5 copy.303
  139.4 0.8 fusion.40
  140.2 0.8 copy_dynamic-update-slice_fusion.1
  141.0 3.2 %fusion.18 = f32[50,4,4,4]{3,2,1,0:T(4,128)S(1)} fusion(f32[50,4,4,4,128]{4,3,2,1,0:T(4,128)} %get-tuple-element.60, f32[50,4,4,4]{3,2,1,0:T(4,128)S(1)} %get-tuple-element.59, pred[50,4,128]{2,1,0:T(4,128)(4,1)S(1)} %or_and_fusion), kind=kLoop, calls=%fused_computation.33 | loop fusion | flops 1635200 | bytes 1689600 | tf_op jit(solution)/shard_map/reduce_sum | solution.py:53
  144.1 0.8 gather_fusion.2
  145.0 0.8 fusion.75
  146.8 0.8 constant_dynamic-slice_fusion.1
  147.6 1.6 collective-permute-start
  149.2 4.7 %fusion.14 = f32[50,4,4,4,128]{4,3,2,1,0:T(4,128)S(1)} fusion(bf16[50,128,4,128,1]{3,2,1,0,4:T(4,128)(2,1)} %bitcast.122, f32[50,4,4,4,128]{4,3,2,1,0:T(4,128)} %get-tuple-element.60, f32[50,4,4,4]{3,2,1,0:T(4,128)} %bitcast.135, f32[50,4,4,4]{3,2,1,0:T(4,128)S(1)} %get-tuple-element.59, pred[50,4,128]{2,1,0:T(4,128)(4,1)S(1)} %copy-done.16), kind=kOutput, calls=%fused_computation.25 | convolution fusion | flops 106905600 | bytes 9881600 | tf_op jit(solution)/shard_map/nasgb,nbah->nasgh/dot_general | solution.py:54
  153.9 2.2 fusion.12
  156.1 1.1 constant_dynamic-slice_fusion.2
  157.4 1.1 copy.308
  158.8 0.5 collective-permute-start.1
  159.3 1.1 fusion.33
  160.5 1.6 collective-permute-start.2
  162.1 1.0 fusion.28
  163.1 0.5 copy.292
  164.0 1.5 collective-permute-done.2
  165.6 2.6 collective-permute-start.4
  168.2 4.1 %collective-permute-done.1 = bf16[2,2,1,8,4,4,4,128]{7,6,5,4,3,2,1,0:T(4,128)(2,1)} collective-permute-done((bf16[2,2,1,8,4,4,4,128]{7,6,5,4,3,2,1,0:T(4,128)(2,1)S(1)}, bf16[2,2,1,8,4,4,4,128]{7,6,5,4,3,2,1,0:T(4,128)(2,1)}, u32[]{:S(2)}, u32[]{:S(2)}) %collective-permute-start.1) | collective-permute-done | bytes 524320 | tf_op jit(solution)/shard_map/ppermute | solution.py:130
  172.3 2.5 fusion.17
  174.9 1.6 collective-permute-start.3
  177.1 4.7 %collective-permute-done.3 = bf16[2,1,1,8,4,4,4,128]{7,6,5,4,3,2,1,0:T(4,128)(2,1)S(1)} collective-permute-done((bf16[2,1,1,8,4,4,4,128]{7,6,5,4,3,2,1,0:T(4,128)(2,1)S(1)}, bf16[2,1,1,8,4,4,4,128]{7,6,5,4,3,2,1,0:T(4,128)(2,1)S(1)}, u32[]{:S(2)}, u32[]{:S(2)}) %collective-permute-start.3) | collective-permute-done | bytes 262176 | tf_op jit(solution)/shard_map/ppermute | solution.py:130
  181.7 0.6 multiply_add_fusion.1
  182.4 2.5 collective-permute-start.5
  185.8 3.9 %collective-permute-done.5 = bf16[1,1,1,8,4,4,4,128]{7,6,5,4,3,2,1,0:T(4,128)(2,1)S(1)} collective-permute-done((bf16[1,1,1,8,4,4,4,128]{7,6,5,4,3,2,1,0:T(4,128)(2,1)S(1)}, bf16[1,1,1,8,4,4,4,128]{7,6,5,4,3,2,1,0:T(4,128)(2,1)S(1)}, u32[]{:S(2)}, u32[]{:S(2)}) %collective-permute-start.5) | collective-permute-done | bytes 131104 | tf_op jit(solution)/shard_map/ppermute | solution.py:130
  189.7 1.6 fusion.38
  191.5 2.0 all_gather.11
  193.5 6.6 %fusion.6 = bf16[2,8,4,2560]{3,1,2,0:T(8,128)(2,1)} fusion(bf16[2,8,4,2048]{3,1,2,0:T(8,128)(2,1)S(1)} %all_gather.11, bf16[2048,2560]{1,0:T(8,128)(2,1)} %param.16), kind=kOutput, calls=%fused_computation.9 | convolution fusion | flops 671252480 | bytes 11075584 | tf_op jit(solution)/shard_map/dot_general | solution.py:229
  200.2 11.6 %reduce-scatter.2.cloned.1.call-done = bf16[1,8,4,2560]{3,1,2,0:T(8,128)(2,1)} async-done(((bf16[2,8,4,2560]{3,1,2,0:T(8,128)(2,1)}), bf16[1,8,4,2560]{3,1,2,0:T(8,128)(2,1)}) %reduce-scatter.2.cloned.1.call-update) | async-done | bytes 163856 | tf_op jit(solution)/shard_map/reduce_scatter | solution.py:233
  211.8 1.8 slice.146
  213.6 1.1 fusion.87
  214.7 41.0 %all-gather.6.cloned.1.call-done = bf16[1,64,4,2560]{3,1,2,0:T(8,128)(2,1)} async-done(((bf16[1,8,4,2560]{3,1,2,0:T(8,128)(2,1)}), bf16[1,64,4,2560]{3,1,2,0:T(8,128)(2,1)}) %all-gather.6.cloned.1.call-update) | async-done | bytes 1310736 | tf_op jit(solution)/shard_map/all_gather | solution.py:236
  255.7 3.4 %copy.315 = bf16[64,4,2560]{2,1,0:T(4,128)(2,1)} copy(bf16[64,4,2560]{2,0,1:T(8,128)(2,1)} %bitcast.132) | data formatting | bytes 2621440
  (97 shorter events, 6.5 us)
Async XLA Ops:
  7.2 55.3 %copy-start = (bf16[2560,512]{1,0:T(8,128)(2,1)S(1)}, bf16[2560,512]{1,0:T(8,128)(2,1)}, u32[]{:S(2)}) copy-start(bf16[2560,512]{1,0:T(8,128)(2,1)} %param.15) | copy-start | bytes 7864324
  7.2 50.0 %all-gather.4.cloned.1.call-start = ((), (), s32[]{:S(2)}) async-start(), calls=%async_computation.1 | async-start | bytes 3932160 | tf_op jit(solution)/shard_map/all_gather | solution.py:171
  15.4 97.6 %all-reduce.3.cloned.1.call-start = ((), (), s32[]{:S(2)}) async-start(), calls=%async_computation.4 | async-start | bytes 6291456
  62.5 3.4 %copy-start.5 = (bf16[512,2560]{1,0:T(8,128)(2,1)S(1)}, bf16[512,2560]{1,0:T(8,128)(2,1)}, u32[]{:S(2)}) copy-start(bf16[512,2560]{1,0:T(8,128)(2,1)} %reshape.465) | copy-start | bytes 7864324
  62.5 3.4 %copy-start.18 = (bf16[2560,512]{1,0:T(8,128)(2,1)S(1)}, bf16[2560,512]{1,0:T(8,128)(2,1)}, u32[]{:S(2)}) copy-start(bf16[2560,512]{1,0:T(8,128)(2,1)} %param.14) | copy-start | bytes 7864324
  83.8 0.7 copy-start.17
  83.8 0.7 copy-start.2
  83.8 127.9 %reduce-scatter.2.cloned.1.call-start = ((), (), s32[]{:S(2)}) async-start(), calls=%async_computation.2 | async-start | bytes 491520 | tf_op jit(solution)/shard_map/reduce_scatter | solution.py:233
  98.8 12.4 %copy-start.20 = (u32[32]{0:T(128)S(1)}, u32[32]{0:T(128)}, u32[]{:S(2)}) copy-start(u32[32]{0:T(128)} %constant.92) | copy-start | bytes 388
  98.8 13.6 %copy-start.19 = (s32[50]{0:T(128)S(1)}, s32[50]{0:T(128)}, u32[]{:S(2)}) copy-start(s32[50]{0:T(128)} %param.19) | copy-start | bytes 604
  113.0 28.0 %copy-start.15 = (pred[50,4,128]{2,1,0:T(4,128)(4,1)}, pred[50,4,128]{2,1,0:T(4,128)(4,1)S(1)}, u32[]{:S(2)}) copy-start(pred[50,4,128]{2,1,0:T(4,128)(4,1)S(1)} %or_and_fusion) | copy-start | bytes 76804
  114.8 1.7 copy-start.3
  137.1 3.1 %copy-start.8 = (f32[1,2,2,2,8,4,4,4]{4,3,2,1,7,6,5,0:T(2,128)S(1)}, f32[1,2,2,2,8,4,4,4]{4,3,2,1,7,6,5,0:T(2,128)}, u32[]{:S(2)}) copy-start(f32[1,2,2,2,8,4,4,4]{4,3,2,1,7,6,5,0:T(2,128)} %stack.10) | copy-start | bytes 49156
  139.4 1.6 copy-start.11
  144.9 1.8 copy-start.6
  145.0 4.2 %copy-start.16 = (pred[50,4,128]{2,1,0:T(4,128)(4,1)S(1)}, pred[50,4,128]{2,1,0:T(4,128)(4,1)}, u32[]{:S(2)}) copy-start(pred[50,4,128]{2,1,0:T(4,128)(4,1)} %copy-done.15) | copy-start | bytes 76804
  146.8 2.4 copy-start.7
  147.6 11.7 %collective-permute-start = (f32[2,2,2,1,8,4,4,4]{4,7,6,5,2,1,3,0:T(4,128)}, f32[2,2,2,1,8,4,4,4]{4,7,6,5,2,1,3,0:T(4,128)S(1)}, u32[]{:S(2)}, u32[]{:S(2)}) collective-permute-start(f32[2,2,2,1,8,4,4,4]{4,7,6,5,2,1,3,0:T(4,128)} %constant_dynamic-slice_fusion.1), channel_id=1, source_target_pairs={{0,1},{1,0},{2,3},{3,2},{4,5},{5,4},{6,7},{7,6},{8,9},{9,8},{10,11... | collective-permute-start | bytes 49160 | tf_op jit(solution)/shard_map/ppermute | solution.py:129
  158.5 13.8 %copy-start.4 = (f32[2,2,1,8,4,4,4,128]{7,3,2,1,0,6,5,4:T(8,128)S(1)}, f32[2,2,1,8,4,4,4,128]{7,3,2,1,0,6,5,4:T(8,128)}, u32[]{:S(2)}) copy-start(f32[2,2,1,8,4,4,4,128]{7,3,2,1,0,6,5,4:T(8,128)} %constant_dynamic-slice_fusion.2) | copy-start | bytes 3145732
  158.8 13.5 %collective-permute-start.1 = (bf16[2,2,1,8,4,4,4,128]{7,6,5,4,3,2,1,0:T(4,128)(2,1)S(1)}, bf16[2,2,1,8,4,4,4,128]{7,6,5,4,3,2,1,0:T(4,128)(2,1)}, u32[]{:S(2)}, u32[]{:S(2)}) collective-permute-start(bf16[2,2,1,8,4,4,4,128]{7,6,5,4,3,2,1,0:T(4,128)(2,1)S(1)} %copy.358), channel_id=1, source_target_pairs={{0,1},{1,0},{2,3},{3,2},{4,5},{5,4},{6,7},{7,6},{8,9},{9,8},{10,11... | collective-permute-start | bytes 1572872 | tf_op jit(solution)/shard_map/ppermute | solution.py:130
  160.5 5.0 %collective-permute-start.2 = (f32[2,2,1,1,8,4,4,4]{4,7,6,5,3,2,1,0:T(4,128)S(1)}, f32[2,2,1,1,8,4,4,4]{4,7,6,5,3,2,1,0:T(4,128)S(1)}, u32[]{:S(2)}, u32[]{:S(2)}) collective-permute-start(f32[2,2,1,1,8,4,4,4]{4,7,6,5,3,2,1,0:T(4,128)S(1)} %get-tuple-element.49), channel_id=1, source_target_pairs={{0,2},{1,3},{2,0},{3,1},{4,6},{5,7},{6,4},{7,5},{8,10},{9,11},{10,... | collective-permute-start | bytes 24584 | tf_op jit(solution)/shard_map/ppermute | solution.py:129
  165.5 2.7 %copy-start.9 = (f32[2,2,1,1,8,4,4,4]{4,7,6,5,3,2,1,0:T(4,128)}, f32[2,2,1,1,8,4,4,4]{4,7,6,5,3,2,1,0:T(4,128)S(1)}, u32[]{:S(2)}) copy-start(f32[2,2,1,1,8,4,4,4]{4,7,6,5,3,2,1,0:T(4,128)S(1)} %collective-permute-done.2) | copy-start | bytes 24580
  165.6 11.4 %collective-permute-start.4 = (f32[2,1,1,1,8,4,4,4]{4,7,6,5,3,2,1,0:T(4,128)S(1)}, f32[2,1,1,1,8,4,4,4]{4,7,6,5,3,2,1,0:T(4,128)S(1)}, u32[]{:S(2)}, u32[]{:S(2)}) collective-permute-start(f32[2,1,1,1,8,4,4,4]{4,7,6,5,3,2,1,0:T(4,128)S(1)} %get-tuple-element.53), channel_id=1, source_target_pairs={{0,4},{1,5},{2,6},{3,7},{4,0},{5,1},{6,2},{7,3},{8,12},{9,13},{10,... | collective-permute-start | bytes 12296 | tf_op jit(solution)/shard_map/ppermute | solution.py:129
  172.3 4.2 %copy-start.10 = (f32[2,2,1,1,8,4,4,4]{4,7,6,5,3,2,1,0:T(4,128)S(1)}, f32[2,2,1,1,8,4,4,4]{4,7,6,5,3,2,1,0:T(4,128)}, u32[]{:S(2)}) copy-start(f32[2,2,1,1,8,4,4,4]{4,7,6,5,3,2,1,0:T(4,128)} %copy-done.9) | copy-start | bytes 24580
  174.8 10.1 %copy-start.12 = (f32[8,4,4,4]{0,3,2,1:T(4,128)S(1)}, f32[8,4,4,4]{0,3,2,1:T(4,128)}, u32[]{:S(2)}) copy-start(f32[8,4,4,4]{0,3,2,1:T(4,128)} %copy-done.11) | copy-start | bytes 6148
  174.8 10.1 %copy-start.14 = (f32[8,4,4,4]{0,3,2,1:T(4,128)S(1)}, f32[8,4,4,4]{0,3,2,1:T(4,128)}, u32[]{:S(2)}) copy-start(f32[8,4,4,4]{0,3,2,1:T(4,128)} %get-tuple-element.51) | copy-start | bytes 6148
  174.8 15.0 %copy-start.13 = (bf16[8,4,4,4,4]{4,3,2,1,0:T(4,128)(2,1)S(1)}, bf16[8,4,4,4,4]{4,3,2,1,0:T(4,128)(2,1)}, u32[]{:S(2)}) copy-start(bf16[8,4,4,4,4]{4,3,2,1,0:T(4,128)(2,1)} %copy.308) | copy-start | bytes 12292
  174.9 6.8 %collective-permute-start.3 = (bf16[2,1,1,8,4,4,4,128]{7,6,5,4,3,2,1,0:T(4,128)(2,1)S(1)}, bf16[2,1,1,8,4,4,4,128]{7,6,5,4,3,2,1,0:T(4,128)(2,1)S(1)}, u32[]{:S(2)}, u32[]{:S(2)}) collective-permute-start(bf16[2,1,1,8,4,4,4,128]{7,6,5,4,3,2,1,0:T(4,128)(2,1)S(1)} %dynamic-slice_convert_fusion.1), channel_id=1, source_target_pairs={{0,2},{1,3},{2,0},{3,1},{4,6},{5,7},{6,4},{7,5},{8,10},{9,11},{10,... | collective-permute-start | bytes 786440 | tf_op jit(solution)/shard_map/ppermute | solution.py:130
  182.4 7.3 %collective-permute-start.5 = (bf16[1,1,1,8,4,4,4,128]{7,6,5,4,3,2,1,0:T(4,128)(2,1)S(1)}, bf16[1,1,1,8,4,4,4,128]{7,6,5,4,3,2,1,0:T(4,128)(2,1)S(1)}, u32[]{:S(2)}, u32[]{:S(2)}) collective-permute-start(bf16[1,1,1,8,4,4,4,128]{7,6,5,4,3,2,1,0:T(4,128)(2,1)S(1)} %dynamic-slice_convert_fusion.2), channel_id=1, source_target_pairs={{0,4},{1,5},{2,6},{3,7},{4,0},{5,1},{6,2},{7,3},{8,12},{9,13},{10,... | collective-permute-start | bytes 393224 | tf_op jit(solution)/shard_map/ppermute | solution.py:130
  200.1 58.9 %copy-start.1 = (bf16[2560,512]{1,0:T(8,128)(2,1)S(1)}, bf16[2560,512]{1,0:T(8,128)(2,1)}, u32[]{:S(2)}) copy-start(bf16[2560,512]{1,0:T(8,128)(2,1)} %param.15) | copy-start | bytes 7864324
  200.1 55.5 %all-gather.6.cloned.1.call-start = ((), (), s32[]{:S(2)}) async-start(), calls=%async_computation.3 | async-start | bytes 1474560 | tf_op jit(solution)/shard_map/all_gather | solution.py:236
Sparse Core Ops, SparseCore 0:
  15.5 41.5 all-gather.3
  84.0 23.1 all-reduce.2
  200.3 11.4 reduce-scatter.1
  213.8 41.7 all-gather.5
where the time goes:
time: 267 us; the launch traced here: 266 us
  waiting for transfers between devices  108 us (40%)
  local copies, waits for them, and re-layouts  62.8 us (24%)
  matrix products  37.9 us (14%)
  other arithmetic  26.2 us (10%)
  between operations  14.9 us (6%)
  starting transfers between devices  10.7 us (4%)
  blocking collectives  4.57 us (2%)
    all_gather x1, waiting for transfers between devices, on_device(): gathered = lax.all_gather(normed, 'col', axis=0, tiled=True)  41.7 us
    all_gather x1, waiting for transfers between devices, on_device(): attended = lax.all_gather(own_out, 'seq', axis=0, tiled=True)  41 us
    dot_general x3, matrix products, on_device(): jnp.dot(piece_rows, matrix, preferred_element_type=jnp.float32)  13.4 us
    ppermute x3, waiting for transfers between devices, seq_merge(): lax.ppermute(send_values.astype(jnp.bfloat16), 'seq', pairs)  12.6 us
    reshape x1, local copies, waits for them, and re-layouts, on_device(): paged_value_cache.reshape(paged_value_cache.shape[0], block_len, heads_kv...  12.4 us
    reshape x1, local copies, waits for them, and re-layouts, on_device(): paged_key_cache.reshape(paged_key_cache.shape[0], block_len, heads_kv, HE...  12.4 us
    reduce_scatter x1, waiting for transfers between devices, on_device(): lax.psum_scatter(partials.astype(jnp.bfloat16), 'col', scatter_dimension=...  11.6 us
    dot_general x1, matrix products, slot_parts(): jnp.einsum('nsagh,nbah->nasgb', slot_queries, key_rows, preferred_element...  7.94 us
  transfers between devices with their start and end apart: 10, of which 7 were waited for; matrix products, arithmetic and copies ran while one was open for 18% of the time, Pallas kernels for 0%

commit v1 on v0

--- a/solution.py
+++ b/solution.py
@@ -233,7 +233,13 @@
     own_out = lax.psum_scatter(
         partials.astype(jnp.bfloat16), "col", scatter_dimension=0, tiled=True
     ).reshape(per, step_count, -1)
-    attended = lax.all_gather(own_out, "seq", axis=0, tiled=True)
+    n_dev = lax.axis_size("seq")
+    moving, blocks = (own_out, [own_out])
+    for _ in range(n_dev - 1):
+        moving = lax.ppermute(moving, "seq", [(i, (i + 1) % n_dev) for i in range(n_dev)])
+        blocks.insert(0, moving)
+    row_of_blocks = jnp.concatenate(blocks, axis=0)
+    attended = jnp.roll(row_of_blocks, (lax.axis_index("seq") + 1) * own_out.shape[0], axis=0)
     return (
         attended,
         current_key.reshape(req_count, step_count, k_width),

time: 267 us -> 283 us (1.060)
  waiting for transfers between devices: 108 us -> 122 us
    ppermute x0 -> x7, waiting for transfers between devices: none -> 54.3 us  [on_device(): lax.ppermute(moving, 'seq', [(i, (i + 1) % n_dev) for i in range(n_dev)])]
    all_gather x1 -> x0, waiting for transfers between devices: 41 us -> none  [on_device(): attended = lax.all_gather(own_out, 'seq', axis=0, tiled=True)]
    unnamed x46 -> x57, local copies, waits for them, and re-layouts: 6.27 us -> 6.1 us
  transfers between devices with their start and end apart: 10 -> 16, of which waited for: 7 -> 13; matrix products, arithmetic and copies ran while one was open for 18% -> 17% of each run, Pallas kernels for 0% -> 0%
where the time goes in v1:
time: 283 us; the launch traced here: 281 us
  waiting for transfers between devices  122 us (43%)
  local copies, waits for them, and re-layouts  64.3 us (23%)
  matrix products  37.9 us (13%)
  other arithmetic  25.5 us (9%)
  between operations  15 us (5%)
  starting transfers between devices  12.1 us (4%)
  blocking collectives  4.57 us (2%)
    ppermute x7, waiting for transfers between devices, on_device(): lax.ppermute(moving, 'seq', [(i, (i + 1) % n_dev) for i in range(n_dev)])  54.3 us
    all_gather x1, waiting for transfers between devices, on_device(): gathered = lax.all_gather(normed, 'col', axis=0, tiled=True)  41.7 us
    dot_general x3, matrix products, on_device(): jnp.dot(piece_rows, matrix, preferred_element_type=jnp.float32)  13.4 us
    ppermute x3, waiting for transfers between devices, seq_merge(): lax.ppermute(send_values.astype(jnp.bfloat16), 'seq', pairs)  12.6 us
    reshape x1, local copies, waits for them, and re-layouts, on_device(): paged_value_cache.reshape(paged_value_cache.shape[0], block_len, heads_kv...  12.4 us
    reshape x1, local copies, waits for them, and re-layouts, on_device(): paged_key_cache.reshape(paged_key_cache.shape[0], block_len, heads_kv, HE...  12.4 us
    reduce_scatter x1, waiting for transfers between devices, on_device(): lax.psum_scatter(partials.astype(jnp.bfloat16), 'col', scatter_dimension=...  11.6 us
    dot_general x1, matrix products, slot_parts(): jnp.einsum('nsagh,nbah->nasgb', slot_queries, key_rows, preferred_element...  7.95 us
  transfers between devices with their start and end apart: 16, of which 13 were waited for; matrix products, arithmetic and copies ran while one was open for 17% of the time, Pallas kernels for 0%

profile of v1, /device:TPU:0, one launch (start us, length us, event | category | flops | bytes accessed | tf_op | source)
XLA Modules:
  0.0 281.3 jit_solution(17020094624939860004)
XLA Ops:
  7.2 2.2 fusion.9
  9.5 2.6 psum.7
  12.2 3.1 %fusion.11 = bf16[64,4,2560]{2,1,0:T(4,128)(2,1)} fusion(bf16[64,4,2560]{2,1,0:T(4,128)(2,1)} %param.11, f32[2560]{0:T(1024)} %param.12, f32[64,4]{1,0:T(8,128)S(1)} %copy.273), kind=kLoop, calls=%fused_computation.16 | loop fusion | flops 2621440 | bytes 2632704 | tf_op jit(solution)/shard_map/convert_element_type | solution.py:168
  15.4 41.7 %all-gather.2.cloned.1.call-done = bf16[128,4,2560]{2,1,0:T(4,128)(2,1)} async-done(((bf16[64,4,2560]{2,1,0:T(4,128)(2,1)}), bf16[128,4,2560]{2,1,0:T(4,128)(2,1)}) %all-gather.2.cloned.1.call-update) | async-done | bytes 2621456 | tf_op jit(solution)/shard_map/all_gather | solution.py:171
  57.1 5.3 %reshape.465 = bf16[512,2560]{1,0:T(8,128)(2,1)} reshape(bf16[128,4,2560]{2,1,0:T(4,128)(2,1)} %all-gather.2.cloned.1.call-done) | data formatting | bytes 5242880 | tf_op jit(solution)/shard_map/reshape | solution.py:172
  62.5 3.4 %convolution_convert_fusion.1 = bf16[512,512]{1,0:T(8,128)(2,1)S(1)} fusion(bf16[512,2560]{1,0:T(8,128)(2,1)} %reshape.465, bf16[2560,512]{1,0:T(8,128)(2,1)S(1)} %copy-done), kind=kOutput, calls=%fused_computation.26 | convolution fusion | flops 1342439424 | bytes 5767168 | tf_op jit(solution)/shard_map/dot_general | solution.py:174
  65.9 1.5 convolution_convert_fusion.2
  67.4 8.5 %convolution_convert_fusion = bf16[512,2048]{1,0:T(8,128)(2,1)S(1)} fusion(bf16[512,2560]{1,0:T(8,128)(2,1)S(1)} %copy-done.5, bf16[2560,2048]{1,0:T(8,128)(2,1)} %param.13), kind=kOutput, calls=%fused_computation.13 | convolution fusion | flops 5369757696 | bytes 15204352 | tf_op jit(solution)/shard_map/dot_general | solution.py:174
  75.9 1.8 pad_maximum_fusion
  77.7 6.1 %convert_element_type.83 = bf16[128,4,3072]{2,1,0:T(4,128)(2,1)} reshape(bf16[512,3072]{1,0:T(8,128)(2,1)} %pad_maximum_fusion) | data formatting | bytes 6291456 | tf_op jit(solution)/shard_map/convert_element_type | solution.py:179
  84.5 0.8 gather_fusion
  85.4 1.1 multiply_cosine_fusion
  86.5 12.4 %reshape.467 = bf16[50,128,4,128]{3,2,1,0:T(4,128)(2,1)} reshape(bf16[50,128,512]{2,1,0:T(8,128)(2,1)} %param.20) | data formatting | bytes 13107200 | tf_op jit(solution)/shard_map/reshape | solution.py:161
  98.9 12.4 %reshape.468 = bf16[50,128,4,128]{3,2,1,0:T(4,128)(2,1)} reshape(bf16[50,128,512]{2,1,0:T(8,128)(2,1)} %param.21) | data formatting | bytes 13107200 | tf_op jit(solution)/shard_map/reshape | solution.py:162
  113.0 1.8 dynamic-slice_convert_fusion
  114.8 0.9 slice_bitcast_fusion.2
  115.8 0.8 copy-done.3
  116.6 1.5 slice.92
  118.1 2.3 reshape.508
  120.4 0.7 fusion.76
  121.8 1.4 pad_maximum_fusion.1
  123.8 2.2 gather_fusion.1
  125.9 8.0 %select_reduce_fusion.1 = (f32[50,4,4,4]{3,2,1,0:T(4,128)S(1)}, f32[50,4,4,4,128]{4,3,2,1,0:T(4,128)}) fusion(pred[50,4,128]{2,1,0:T(4,128)(4,1)S(1)} %or_and_fusion, bf16[50,4,4,4,128]{4,3,1,2,0:T(4,128)(2,1)} %gather_fusion.1, bf16[50,128,4,128,1]{3,2,1,0,4:T(4,128)(2,1)} %bitcast.125), kind=kOutput, calls=%fused_computation.23 | convolution fusion | flops 106083200 | bytes 9049600 | tf_op jit(solution)/shard_map/nsagh,nbah->nasgb/dot_general | solution.py:37
  133.9 1.3 select_reduce_fusion
  135.1 1.1 stack.10
  137.5 1.2 fusion.36
  139.4 0.8 fusion.40
  140.2 1.7 copy_dynamic-update-slice_fusion.1
  141.9 3.2 %fusion.18 = f32[50,4,4,4]{3,2,1,0:T(4,128)S(1)} fusion(f32[50,4,4,4,128]{4,3,2,1,0:T(4,128)} %get-tuple-element.60, f32[50,4,4,4]{3,2,1,0:T(4,128)S(1)} %get-tuple-element.59, pred[50,4,128]{2,1,0:T(4,128)(4,1)S(1)} %or_and_fusion), kind=kLoop, calls=%fused_computation.33 | loop fusion | flops 1635200 | bytes 1689600 | tf_op jit(solution)/shard_map/reduce_sum | solution.py:53
  145.1 0.8 gather_fusion.2
  147.0 0.8 copy_dynamic-update-slice_fusion
  147.7 1.7 constant_dynamic-slice_fusion.2
  149.4 1.6 collective-permute-start
  151.0 4.7 %fusion.14 = f32[50,4,4,4,128]{4,3,2,1,0:T(4,128)S(1)} fusion(bf16[50,128,4,128,1]{3,2,1,0,4:T(4,128)(2,1)} %bitcast.124, f32[50,4,4,4,128]{4,3,2,1,0:T(4,128)} %get-tuple-element.60, f32[50,4,4,4]{3,2,1,0:T(4,128)S(1)} %bitcast.137, f32[50,4,4,4]{3,2,1,0:T(4,128)S(1)} %get-tuple-element.59, pred[50,4,128]{2,1,0:T(4,128)(4,1)S(1)} %copy-done.14), kind=kOutput, calls=%fused_computation.25 | convolution fusion | flops 106905600 | bytes 9881600 | tf_op jit(solution)/shard_map/nasgb,nbah->nasgh/dot_general | solution.py:54
  155.8 2.2 fusion.12
  157.9 1.1 constant_dynamic-slice_fusion.3
  159.2 1.1 copy.308
  161.1 1.1 fusion.33
  162.3 1.6 collective-permute-start.2
  163.9 1.0 fusion.28
  165.8 1.5 collective-permute-done.2
  167.4 2.6 collective-permute-start.4
  170.0 4.1 %collective-permute-done.1 = bf16[2,2,1,8,4,4,4,128]{7,6,5,4,3,2,1,0:T(4,128)(2,1)} collective-permute-done((bf16[2,2,1,8,4,4,4,128]{7,6,5,4,3,2,1,0:T(4,128)(2,1)S(1)}, bf16[2,2,1,8,4,4,4,128]{7,6,5,4,3,2,1,0:T(4,128)(2,1)}, u32[]{:S(2)}, u32[]{:S(2)}) %collective-permute-start.1) | collective-permute-done | bytes 524320 | tf_op jit(solution)/shard_map/ppermute | solution.py:130
  174.1 2.5 fusion.17
  176.7 1.6 collective-permute-start.3
  178.9 4.7 %collective-permute-done.3 = bf16[2,1,1,8,4,4,4,128]{7,6,5,4,3,2,1,0:T(4,128)(2,1)S(1)} collective-permute-done((bf16[2,1,1,8,4,4,4,128]{7,6,5,4,3,2,1,0:T(4,128)(2,1)S(1)}, bf16[2,1,1,8,4,4,4,128]{7,6,5,4,3,2,1,0:T(4,128)(2,1)S(1)}, u32[]{:S(2)}, u32[]{:S(2)}) %collective-permute-start.3) | collective-permute-done | bytes 262176 | tf_op jit(solution)/shard_map/ppermute | solution.py:130
  183.5 0.6 multiply_add_fusion.1
  184.2 2.5 collective-permute-start.5
  187.6 3.9 %collective-permute-done.5 = bf16[1,1,1,8,4,4,4,128]{7,6,5,4,3,2,1,0:T(4,128)(2,1)S(1)} collective-permute-done((bf16[1,1,1,8,4,4,4,128]{7,6,5,4,3,2,1,0:T(4,128)(2,1)S(1)}, bf16[1,1,1,8,4,4,4,128]{7,6,5,4,3,2,1,0:T(4,128)(2,1)S(1)}, u32[]{:S(2)}, u32[]{:S(2)}) %collective-permute-start.5) | collective-permute-done | bytes 131104 | tf_op jit(solution)/shard_map/ppermute | solution.py:130
  191.5 1.6 fusion.38
  193.3 2.0 all_gather.8
  195.3 6.6 %fusion.6 = bf16[2,8,4,2560]{3,1,2,0:T(8,128)(2,1)} fusion(bf16[2,8,4,2048]{3,1,2,0:T(8,128)(2,1)S(1)} %all_gather.8, bf16[2048,2560]{1,0:T(8,128)(2,1)} %param.16), kind=kOutput, calls=%fused_computation.9 | convolution fusion | flops 671252480 | bytes 11075584 | tf_op jit(solution)/shard_map/dot_general | solution.py:229
  201.9 11.6 %reduce-scatter.2.cloned.1.call-done = bf16[1,8,4,2560]{3,1,2,0:T(8,128)(2,1)} async-done(((bf16[2,8,4,2560]{3,1,2,0:T(8,128)(2,1)}), bf16[1,8,4,2560]{3,1,2,0:T(8,128)(2,1)}) %reduce-scatter.2.cloned.1.call-update) | async-done | bytes 163856 | tf_op jit(solution)/shard_map/reduce_scatter | solution.py:233
  213.6 1.5 collective-permute-start.6
  215.0 7.4 %collective-permute-done.6 = bf16[8,4,2560]{2,0,1:T(8,128)(2,1)S(1)} collective-permute-done((bf16[8,4,2560]{2,0,1:T(8,128)(2,1)}, bf16[8,4,2560]{2,0,1:T(8,128)(2,1)S(1)}, u32[]{:S(2)}, u32[]{:S(2)}) %collective-permute-start.6) | collective-permute-done | bytes 163872 | tf_op jit(solution)/shard_map/ppermute | solution.py:239
  222.4 8.0 %collective-permute-done.7 = bf16[8,4,2560]{2,0,1:T(8,128)(2,1)S(1)} collective-permute-done((bf16[8,4,2560]{2,0,1:T(8,128)(2,1)S(1)}, bf16[8,4,2560]{2,0,1:T(8,128)(2,1)S(1)}, u32[]{:S(2)}, u32[]{:S(2)}) %collective-permute-start.7) | collective-permute-done | bytes 163872 | tf_op jit(solution)/shard_map/ppermute | solution.py:239
  230.4 8.0 %collective-permute-done.8 = bf16[8,4,2560]{2,0,1:T(8,128)(2,1)S(1)} collective-permute-done((bf16[8,4,2560]{2,0,1:T(8,128)(2,1)S(1)}, bf16[8,4,2560]{2,0,1:T(8,128)(2,1)S(1)}, u32[]{:S(2)}, u32[]{:S(2)}) %collective-permute-start.8) | collective-permute-done | bytes 163872 | tf_op jit(solution)/shard_map/ppermute | solution.py:239
  238.4 8.0 %collective-permute-done.9 = bf16[8,4,2560]{2,0,1:T(8,128)(2,1)S(1)} collective-permute-done((bf16[8,4,2560]{2,0,1:T(8,128)(2,1)S(1)}, bf16[8,4,2560]{2,0,1:T(8,128)(2,1)S(1)}, u32[]{:S(2)}, u32[]{:S(2)}) %collective-permute-start.9) | collective-permute-done | bytes 163872 | tf_op jit(solution)/shard_map/ppermute | solution.py:239
  246.5 8.3 %collective-permute-done.10 = bf16[8,4,2560]{2,0,1:T(8,128)(2,1)S(1)} collective-permute-done((bf16[8,4,2560]{2,0,1:T(8,128)(2,1)S(1)}, bf16[8,4,2560]{2,0,1:T(8,128)(2,1)S(1)}, u32[]{:S(2)}, u32[]{:S(2)}) %collective-permute-start.10) | collective-permute-done | bytes 163872 | tf_op jit(solution)/shard_map/ppermute | solution.py:239
  254.8 9.4 %collective-permute-done.11 = bf16[8,4,2560]{2,0,1:T(8,128)(2,1)S(1)} collective-permute-done((bf16[8,4,2560]{2,0,1:T(8,128)(2,1)S(1)}, bf16[8,4,2560]{2,0,1:T(8,128)(2,1)S(1)}, u32[]{:S(2)}, u32[]{:S(2)}) %collective-permute-start.11) | collective-permute-done | bytes 163872 | tf_op jit(solution)/shard_map/ppermute | solution.py:239
  264.2 1.8 slice.146
  266.0 1.1 fusion.87
  267.1 5.1 %collective-permute-done.12 = bf16[8,4,2560]{2,0,1:T(8,128)(2,1)S(1)} collective-permute-done((bf16[8,4,2560]{2,0,1:T(8,128)(2,1)S(1)}, bf16[8,4,2560]{2,0,1:T(8,128)(2,1)S(1)}, u32[]{:S(2)}, u32[]{:S(2)}) %collective-permute-start.12) | collective-permute-done | bytes 163872 | tf_op jit(solution)/shard_map/ppermute | solution.py:239
  272.7 2.1 copy.315
  (121 shorter events, 10.4 us)
Async XLA Ops:
  7.2 55.3 %copy-start = (bf16[2560,512]{1,0:T(8,128)(2,1)S(1)}, bf16[2560,512]{1,0:T(8,128)(2,1)}, u32[]{:S(2)}) copy-start(bf16[2560,512]{1,0:T(8,128)(2,1)} %param.15) | copy-start | bytes 7864324
  7.2 50.0 %all-gather.2.cloned.1.call-start = ((), (), s32[]{:S(2)}) async-start(), calls=%async_computation.1 | async-start | bytes 3932160 | tf_op jit(solution)/shard_map/all_gather | solution.py:171
  15.4 97.6 %all-reduce.3.cloned.1.call-start = ((), (), s32[]{:S(2)}) async-start(), calls=%async_computation.3 | async-start | bytes 6291456
  62.5 3.4 %copy-start.5 = (bf16[512,2560]{1,0:T(8,128)(2,1)S(1)}, bf16[512,2560]{1,0:T(8,128)(2,1)}, u32[]{:S(2)}) copy-start(bf16[512,2560]{1,0:T(8,128)(2,1)} %reshape.465) | copy-start | bytes 7864324
  62.5 3.4 %copy-start.16 = (bf16[2560,512]{1,0:T(8,128)(2,1)S(1)}, bf16[2560,512]{1,0:T(8,128)(2,1)}, u32[]{:S(2)}) copy-start(bf16[2560,512]{1,0:T(8,128)(2,1)} %param.14) | copy-start | bytes 7864324
  83.8 0.7 copy-start.15
  83.8 0.7 copy-start.2
  83.8 129.7 %reduce-scatter.2.cloned.1.call-start = ((), (), s32[]{:S(2)}) async-start(), calls=%async_computation.2 | async-start | bytes 491520 | tf_op jit(solution)/shard_map/reduce_scatter | solution.py:233
  98.9 12.4 %copy-start.18 = (u32[32]{0:T(128)S(1)}, u32[32]{0:T(128)}, u32[]{:S(2)}) copy-start(u32[32]{0:T(128)} %constant.111) | copy-start | bytes 388
  98.9 13.6 %copy-start.17 = (s32[50]{0:T(128)S(1)}, s32[50]{0:T(128)}, u32[]{:S(2)}) copy-start(s32[50]{0:T(128)} %param.19) | copy-start | bytes 604
  113.0 29.0 %copy-start.13 = (pred[50,4,128]{2,1,0:T(4,128)(4,1)}, pred[50,4,128]{2,1,0:T(4,128)(4,1)S(1)}, u32[]{:S(2)}) copy-start(pred[50,4,128]{2,1,0:T(4,128)(4,1)S(1)} %or_and_fusion) | copy-start | bytes 76804
  114.8 1.7 copy-start.3
  139.4 2.6 copy-start.9
  145.1 5.9 %copy-start.14 = (pred[50,4,128]{2,1,0:T(4,128)(4,1)S(1)}, pred[50,4,128]{2,1,0:T(4,128)(4,1)}, u32[]{:S(2)}) copy-start(pred[50,4,128]{2,1,0:T(4,128)(4,1)} %copy-done.13) | copy-start | bytes 76804
  149.4 11.7 %collective-permute-start = (f32[2,2,2,1,8,4,4,4]{4,7,6,5,2,1,3,0:T(4,128)}, f32[2,2,2,1,8,4,4,4]{4,7,6,5,2,1,3,0:T(4,128)S(1)}, u32[]{:S(2)}, u32[]{:S(2)}) collective-permute-start(f32[2,2,2,1,8,4,4,4]{4,7,6,5,2,1,3,0:T(4,128)} %constant_dynamic-slice_fusion.2), channel_id=1, source_target_pairs={{0,1},{1,0},{2,3},{3,2},{4,5},{5,4},{6,7},{7,6},{8,9},{9,8},{10,11... | collective-permute-start | bytes 49160 | tf_op jit(solution)/shard_map/ppermute | solution.py:129
  159.2 14.9 %copy-start.4 = (f32[2,2,1,8,4,4,4,128]{7,3,2,1,0,6,5,4:T(8,128)S(1)}, f32[2,2,1,8,4,4,4,128]{7,3,2,1,0,6,5,4:T(8,128)}, u32[]{:S(2)}) copy-start(f32[2,2,1,8,4,4,4,128]{7,3,2,1,0,6,5,4:T(8,128)} %constant_dynamic-slice_fusion.3) | copy-start | bytes 3145732
  160.6 13.5 %collective-permute-start.1 = (bf16[2,2,1,8,4,4,4,128]{7,6,5,4,3,2,1,0:T(4,128)(2,1)S(1)}, bf16[2,2,1,8,4,4,4,128]{7,6,5,4,3,2,1,0:T(4,128)(2,1)}, u32[]{:S(2)}, u32[]{:S(2)}) collective-permute-start(bf16[2,2,1,8,4,4,4,128]{7,6,5,4,3,2,1,0:T(4,128)(2,1)S(1)} %copy.358), channel_id=1, source_target_pairs={{0,1},{1,0},{2,3},{3,2},{4,5},{5,4},{6,7},{7,6},{8,9},{9,8},{10,11... | collective-permute-start | bytes 1572872 | tf_op jit(solution)/shard_map/ppermute | solution.py:130
  162.3 5.0 %collective-permute-start.2 = (f32[2,2,1,1,8,4,4,4]{4,7,6,5,3,2,1,0:T(4,128)S(1)}, f32[2,2,1,1,8,4,4,4]{4,7,6,5,3,2,1,0:T(4,128)S(1)}, u32[]{:S(2)}, u32[]{:S(2)}) collective-permute-start(f32[2,2,1,1,8,4,4,4]{4,7,6,5,3,2,1,0:T(4,128)S(1)} %get-tuple-element.49), channel_id=1, source_target_pairs={{0,2},{1,3},{2,0},{3,1},{4,6},{5,7},{6,4},{7,5},{8,10},{9,11},{10,... | collective-permute-start | bytes 24584 | tf_op jit(solution)/shard_map/ppermute | solution.py:129
  167.3 2.7 copy-start.7
  167.4 19.3 %copy-start.10 = (f32[8,4,4,4]{0,3,2,1:T(4,128)S(1)}, f32[8,4,4,4]{0,3,2,1:T(4,128)}, u32[]{:S(2)}) copy-start(f32[8,4,4,4]{0,3,2,1:T(4,128)} %copy-done.9) | copy-start | bytes 6148
  167.4 19.2 %copy-start.12 = (f32[8,4,4,4]{0,3,2,1:T(4,128)S(1)}, f32[8,4,4,4]{0,3,2,1:T(4,128)}, u32[]{:S(2)}) copy-start(f32[8,4,4,4]{0,3,2,1:T(4,128)} %get-tuple-element.51) | copy-start | bytes 6148
  167.4 11.4 %collective-permute-start.4 = (f32[2,1,1,1,8,4,4,4]{4,7,6,5,3,2,1,0:T(4,128)S(1)}, f32[2,1,1,1,8,4,4,4]{4,7,6,5,3,2,1,0:T(4,128)S(1)}, u32[]{:S(2)}, u32[]{:S(2)}) collective-permute-start(f32[2,1,1,1,8,4,4,4]{4,7,6,5,3,2,1,0:T(4,128)S(1)} %get-tuple-element.53), channel_id=1, source_target_pairs={{0,4},{1,5},{2,6},{3,7},{4,0},{5,1},{6,2},{7,3},{8,12},{9,13},{10,... | collective-permute-start | bytes 12296 | tf_op jit(solution)/shard_map/ppermute | solution.py:129
  174.1 4.2 %copy-start.8 = (f32[2,2,1,1,8,4,4,4]{4,7,6,5,3,2,1,0:T(4,128)S(1)}, f32[2,2,1,1,8,4,4,4]{4,7,6,5,3,2,1,0:T(4,128)}, u32[]{:S(2)}) copy-start(f32[2,2,1,1,8,4,4,4]{4,7,6,5,3,2,1,0:T(4,128)} %copy-done.7) | copy-start | bytes 24580
  176.6 15.0 %copy-start.11 = (bf16[8,4,4,4,4]{4,3,2,1,0:T(4,128)(2,1)S(1)}, bf16[8,4,4,4,4]{4,3,2,1,0:T(4,128)(2,1)}, u32[]{:S(2)}) copy-start(bf16[8,4,4,4,4]{4,3,2,1,0:T(4,128)(2,1)} %copy.308) | copy-start | bytes 12292
  176.7 6.8 %collective-permute-start.3 = (bf16[2,1,1,8,4,4,4,128]{7,6,5,4,3,2,1,0:T(4,128)(2,1)S(1)}, bf16[2,1,1,8,4,4,4,128]{7,6,5,4,3,2,1,0:T(4,128)(2,1)S(1)}, u32[]{:S(2)}, u32[]{:S(2)}) collective-permute-start(bf16[2,1,1,8,4,4,4,128]{7,6,5,4,3,2,1,0:T(4,128)(2,1)S(1)} %dynamic-slice_convert_fusion.1), channel_id=1, source_target_pairs={{0,2},{1,3},{2,0},{3,1},{4,6},{5,7},{6,4},{7,5},{8,10},{9,11},{10,... | collective-permute-start | bytes 786440 | tf_op jit(solution)/shard_map/ppermute | solution.py:130
  184.2 7.3 %collective-permute-start.5 = (bf16[1,1,1,8,4,4,4,128]{7,6,5,4,3,2,1,0:T(4,128)(2,1)S(1)}, bf16[1,1,1,8,4,4,4,128]{7,6,5,4,3,2,1,0:T(4,128)(2,1)S(1)}, u32[]{:S(2)}, u32[]{:S(2)}) collective-permute-start(bf16[1,1,1,8,4,4,4,128]{7,6,5,4,3,2,1,0:T(4,128)(2,1)S(1)} %dynamic-slice_convert_fusion.2), channel_id=1, source_target_pairs={{0,4},{1,5},{2,6},{3,7},{4,0},{5,1},{6,2},{7,3},{8,12},{9,13},{10,... | collective-permute-start | bytes 393224 | tf_op jit(solution)/shard_map/ppermute | solution.py:130
  213.6 58.8 %copy-start.6 = (bf16[1,8,4,2560]{3,1,2,0:T(8,128)(2,1)S(1)}, bf16[1,8,4,2560]{3,1,2,0:T(8,128)(2,1)}, u32[]{:S(2)}) copy-start(bf16[1,8,4,2560]{3,1,2,0:T(8,128)(2,1)} %reduce-scatter.2.cloned.1.call-done) | copy-start | bytes 491524
  213.6 8.9 %collective-permute-start.6 = (bf16[8,4,2560]{2,0,1:T(8,128)(2,1)}, bf16[8,4,2560]{2,0,1:T(8,128)(2,1)S(1)}, u32[]{:S(2)}, u32[]{:S(2)}) collective-permute-start(bf16[8,4,2560]{2,0,1:T(8,128)(2,1)} %bitcast.134), channel_id=1, source_target_pairs={{0,1},{1,2},{2,3},{3,4},{4,5},{5,6},{6,7},{7,0},{8,9},{9,10},{10,1... | collective-permute-start | bytes 491528 | tf_op jit(solution)/shard_map/ppermute | solution.py:239
  222.4 8.0 %collective-permute-start.7 = (bf16[8,4,2560]{2,0,1:T(8,128)(2,1)S(1)}, bf16[8,4,2560]{2,0,1:T(8,128)(2,1)S(1)}, u32[]{:S(2)}, u32[]{:S(2)}) collective-permute-start(bf16[8,4,2560]{2,0,1:T(8,128)(2,1)S(1)} %collective-permute-done.6), channel_id=1, source_target_pairs={{0,1},{1,2},{2,3},{3,4},{4,5},{5,6},{6,7},{7,0},{8,9},{9,10},{10,1... | collective-permute-start | bytes 491528 | tf_op jit(solution)/shard_map/ppermute | solution.py:239
  230.4 8.0 %collective-permute-start.8 = (bf16[8,4,2560]{2,0,1:T(8,128)(2,1)S(1)}, bf16[8,4,2560]{2,0,1:T(8,128)(2,1)S(1)}, u32[]{:S(2)}, u32[]{:S(2)}) collective-permute-start(bf16[8,4,2560]{2,0,1:T(8,128)(2,1)S(1)} %collective-permute-done.7), channel_id=1, source_target_pairs={{0,1},{1,2},{2,3},{3,4},{4,5},{5,6},{6,7},{7,0},{8,9},{9,10},{10,1... | collective-permute-start | bytes 491528 | tf_op jit(solution)/shard_map/ppermute | solution.py:239
  238.4 8.0 %collective-permute-start.9 = (bf16[8,4,2560]{2,0,1:T(8,128)(2,1)S(1)}, bf16[8,4,2560]{2,0,1:T(8,128)(2,1)S(1)}, u32[]{:S(2)}, u32[]{:S(2)}) collective-permute-start(bf16[8,4,2560]{2,0,1:T(8,128)(2,1)S(1)} %collective-permute-done.8), channel_id=1, source_target_pairs={{0,1},{1,2},{2,3},{3,4},{4,5},{5,6},{6,7},{7,0},{8,9},{9,10},{10,1... | collective-permute-start | bytes 491528 | tf_op jit(solution)/shard_map/ppermute | solution.py:239
  246.5 8.3 %collective-permute-start.10 = (bf16[8,4,2560]{2,0,1:T(8,128)(2,1)S(1)}, bf16[8,4,2560]{2,0,1:T(8,128)(2,1)S(1)}, u32[]{:S(2)}, u32[]{:S(2)}) collective-permute-start(bf16[8,4,2560]{2,0,1:T(8,128)(2,1)S(1)} %collective-permute-done.9), channel_id=1, source_target_pairs={{0,1},{1,2},{2,3},{3,4},{4,5},{5,6},{6,7},{7,0},{8,9},{9,10},{10,1... | collective-permute-start | bytes 491528 | tf_op jit(solution)/shard_map/ppermute | solution.py:239
  254.8 9.4 %collective-permute-start.11 = (bf16[8,4,2560]{2,0,1:T(8,128)(2,1)S(1)}, bf16[8,4,2560]{2,0,1:T(8,128)(2,1)S(1)}, u32[]{:S(2)}, u32[]{:S(2)}) collective-permute-start(bf16[8,4,2560]{2,0,1:T(8,128)(2,1)S(1)} %collective-permute-done.10), channel_id=1, source_target_pairs={{0,1},{1,2},{2,3},{3,4},{4,5},{5,6},{6,7},{7,0},{8,9},{9,10},{10,1... | collective-permute-start | bytes 491528 | tf_op jit(solution)/shard_map/ppermute | solution.py:239
  264.2 8.0 %collective-permute-start.12 = (bf16[8,4,2560]{2,0,1:T(8,128)(2,1)S(1)}, bf16[8,4,2560]{2,0,1:T(8,128)(2,1)S(1)}, u32[]{:S(2)}, u32[]{:S(2)}) collective-permute-start(bf16[8,4,2560]{2,0,1:T(8,128)(2,1)S(1)} %collective-permute-done.11), channel_id=1, source_target_pairs={{0,1},{1,2},{2,3},{3,4},{4,5},{5,6},{6,7},{7,0},{8,9},{9,10},{10,1... | collective-permute-start | bytes 491528 | tf_op jit(solution)/shard_map/ppermute | solution.py:239
  272.5 2.2 copy-start.1
Sparse Core Ops, SparseCore 0:
  15.5 41.5 all-gather.1
  84.0 23.2 all-reduce.2
  202.1 11.4 reduce-scatter.1
